TPU v7x, 512 devices: a whole 4x4x16 slice. The times are simulated.
512 devices in a mesh: pipe: 32 (over z, x_hi), tensor: 16 (over x_lo, y, core).
Axes of the slice: x: 4 (x_hi: 2, x_lo: 2; x = x_hi * 2 + x_lo), y: 4, z: 16, core: 2. Of those that a mesh axis runs over, the one named last changes fastest.
Arguments:
- x_saved: bfloat16 [32, 2, 4096, 128], P('pipe', None, 'tensor'), may hold values from -6 to 6
- seed_grad: bfloat16 [32, 2, 4096, 128], P('pipe', None, 'tensor'), may hold values from -6 to 6
- gate_blocks: bfloat16 [32, 16, 7, 20, 4096], P('pipe', 'tensor'), may hold values from -0.1875 to 0.1875
- up_blocks: bfloat16 [32, 16, 7, 20, 4096], P('pipe', 'tensor'), may hold values from -0.1875 to 0.1875
- down_blocks: bfloat16 [32, 16, 7, 20, 4096], P('pipe', 'tensor'), may hold values from -0.1875 to 0.1875
- gate_rows: int32 [32, 16, 7, 20], P('pipe', 'tensor'), may hold values from -1 to 63, as said below
- down_rows: int32 [32, 16, 7, 20], P('pipe', 'tensor'), may hold values from -1 to 63, as said below
Outputs:
- grad_input: bfloat16 [32, 2, 4096, 128], P('pipe', None, 'tensor')
Inputs may be any that keep to these rules, and one draw needn't show every extreme that they name: `gate_rows`: in one column of tiles the non-negative entries are distinct and come before the -1 entries. All columns of one tensor shard of one section hold the same number of kept tiles, from 12 to 20, and in every section one shard holds 20 in every column. `down_rows`: as for gate_rows, drawn independently.
All inputs are finite; a program needn't handle non-finite values.
Results may differ from a plain program's by a relative error of at most 0.007.
Values may be sent and summed in bfloat16 or wider, within the bound.
No kernel may reach another device: no remote copies, remote signals or barrier semaphores. Data moves between devices by JAX's collectives and lax.ppermute only.
A program may use at most 128 MiB of HBM per device.

v0:
```python
import jax
import jax.numpy as jnp
from jax import lax
from jax.sharding import PartitionSpec as P

BLK = 64


def partner_2(x, axis, distance):
    return lax.ppermute(x, axis, [(i, i ^ 1 << distance) for i in range(lax.axis_size(axis))])


def from_behind(block, axis, distance):
    devices = range(lax.axis_size(axis))
    route = [(i - distance, i) for i in devices if i - distance in devices]
    return lax.ppermute(block, axis, route)


def gather_tiles(source, row_ids):
    columns, slot_depth = row_ids.shape
    filled = (row_ids >= 0).reshape(-1)
    picked = jnp.take(source, jnp.maximum(row_ids, 0).reshape(-1), axis=0)
    picked = jnp.where(filled[:, None, None], picked, jnp.zeros_like(picked))
    return picked.reshape(columns, slot_depth, source.shape[1], source.shape[2])


def layer_branch(x_full, cot_full, paired_grid, down_grid, gate_ids, down_ids):
    row_blocks = x_full.shape[0] // BLK
    tokens_now = x_full.shape[1]
    columns, slot_depth = gate_ids.shape
    x_picked = gather_tiles(x_full.reshape(row_blocks, BLK, tokens_now), gate_ids)
    both_values = jnp.einsum(
        "crkj,crkt->cjt", paired_grid, x_picked, preferred_element_type=jnp.float32
    )
    gate_value = both_values[:, :BLK]
    up_value = both_values[:, BLK:]
    cot_picked = gather_tiles(cot_full.reshape(row_blocks, BLK, tokens_now), down_ids)
    d_hidden = jnp.einsum(
        "crjk,crkt->cjt", down_grid, cot_picked, preferred_element_type=jnp.float32
    )
    sigmoid_gate = jax.nn.sigmoid(gate_value)
    d_gate = (
        d_hidden * up_value * sigmoid_gate * (1.0 + gate_value * (1.0 - sigmoid_gate))
    ).astype(jnp.bfloat16)
    d_up = (d_hidden * gate_value * sigmoid_gate).astype(jnp.bfloat16)
    d_both = jnp.concatenate([d_gate, d_up], axis=1)
    per_slot = jnp.einsum("crkj,cjt->crkt", paired_grid, d_both, preferred_element_type=jnp.float32)
    segment_ids = jnp.where(gate_ids >= 0, gate_ids, row_blocks).reshape(-1)
    summed = jax.ops.segment_sum(
        per_slot.reshape(columns * slot_depth, BLK, tokens_now),
        segment_ids,
        num_segments=row_blocks + 1,
    )
    return summed[:row_blocks].reshape(row_blocks * BLK, tokens_now)


def per_device(x_saved, seed_grad, gate_blocks, up_blocks, down_blocks, gate_rows, down_rows):
    pipe_index = lax.axis_index("pipe")
    pair_half = pipe_index % 2
    last_section = pipe_index // 2 == lax.axis_size("pipe") // 2 - 1
    own_parts = (gate_blocks, up_blocks, down_blocks, gate_rows, down_rows)
    partner = partner_2((gate_blocks, up_blocks, down_blocks, gate_rows, down_rows), "pipe", 0)
    joined = []
    for own_part, theirs in zip(own_parts, partner):
        first_half = jnp.where(pair_half == 0, own_part, theirs)
        second_half = jnp.where(pair_half == 0, theirs, own_part)
        joined.append(jnp.concatenate([first_half[0, 0], second_half[0, 0]], axis=0))
    gate_set, up_set, down_set, gate_ids, down_ids = joined
    columns, slot_depth = gate_ids.shape
    tile_shape = (columns, slot_depth, BLK, BLK)
    paired_grid = jnp.concatenate(
        [gate_set.reshape(tile_shape), up_set.reshape(tile_shape)], axis=3
    )
    down_grid = down_set.reshape(tile_shape)
    panel_rows = x_saved.shape[2]
    micro_total = x_saved.shape[1]
    arrived = None
    grads = []
    for micro_step in range(micro_total):
        x_panel = x_saved[0, micro_step]
        seed_panel = seed_grad[0, micro_step]
        x_full, cot_full = (
            lax.all_gather(x_panel, "tensor", axis=0, tiled=True),
            lax.all_gather(seed_panel, "tensor", axis=0, tiled=True),
        )
        if micro_step > 0:
            cot_full = jnp.where(last_section, cot_full, arrived)
        branch = layer_branch(x_full, cot_full, paired_grid, down_grid, gate_ids, down_ids)
        summed = lax.psum(branch, "tensor")
        grad_full = (cot_full.astype(jnp.float32) + summed).astype(jnp.bfloat16)
        grad_panel = lax.dynamic_slice_in_dim(
            grad_full, lax.axis_index("tensor") * panel_rows, panel_rows, 0
        )
        if micro_step + 1 < micro_total:
            arrived = from_behind(grad_full, "pipe", -2)
        grads.append(grad_panel)
    return jnp.stack(grads)[None]


def solution(mesh):
    return jax.shard_map(
        per_device,
        mesh=mesh,
        in_specs=(
            P("pipe", None, "tensor", None),
            P("pipe", None, "tensor", None),
            P("pipe", "tensor", None, None, None),
            P("pipe", "tensor", None, None, None),
            P("pipe", "tensor", None, None, None),
            P("pipe", "tensor", None, None),
            P("pipe", "tensor", None, None),
        ),
        out_specs=P("pipe", None, "tensor", None),
        check_vma=False,
    )
```

profile of v0, /device:TPU:1, one launch (start us, length us, event | category | flops | bytes accessed | tf_op | source)
XLA Modules:
  0.0 603.3 jit_solution(8425488830314063497)
XLA Ops:
  9.6 5.5 collective-permute-start
  17.0 4.9 collective-permute-start.3
  23.8 4.9 collective-permute-start.1
  31.7 19.6 %collective-permute-done.3 = bf16[1,1,7,20,4096]{4,2,3,1,0:T(8,128)(2,1)S(1)} collective-permute-done((bf16[1,1,7,20,4096]{4,2,3,1,0:T(8,128)(2,1)}, bf16[1,1,7,20,4096]{4,2,3,1,0:T(8,128)(2,1)S(1)}, u32[]{:S(2)}, u32[]{:S(2)}) %collective-permute-start.3) | collective-permute-done | bytes 1146912 | tf_op jit(solution)/shard_map/ppermute | solution.py:10
  51.3 29.8 %collective-permute-done.2 = bf16[1,1,7,20,4096]{4,2,3,1,0:T(8,128)(2,1)S(1)} collective-permute-done((bf16[1,1,7,20,4096]{4,2,3,1,0:T(8,128)(2,1)}, bf16[1,1,7,20,4096]{4,2,3,1,0:T(8,128)(2,1)S(1)}, u32[]{:S(2)}, u32[]{:S(2)}) %collective-permute-start.2) | collective-permute-done | bytes 1146912 | tf_op jit(solution)/shard_map/ppermute | solution.py:10
  81.1 4.3 broadcast_select_fusion.1
  85.4 3.6 concatenate.47
  89.0 4.5 concatenate.46
  93.5 19.2 %collective-permute-done.1 = bf16[1,1,7,20,4096]{4,2,3,1,0:T(8,128)(2,1)} collective-permute-done((bf16[1,1,7,20,4096]{4,2,3,1,0:T(8,128)(2,1)}, bf16[1,1,7,20,4096]{4,2,3,1,0:T(8,128)(2,1)}, u32[]{:S(2)}, u32[]{:S(2)}) %collective-permute-start.1) | collective-permute-done | bytes 1146912 | tf_op jit(solution)/shard_map/ppermute | solution.py:10
  112.7 3.3 broadcast_select_fusion.5
  116.1 4.5 concatenate.44
  120.6 4.5 concatenate.43
  125.1 4.5 concatenate.51
  129.7 4.5 concatenate.50
  134.2 6.4 %maximum_maximum_fusion = bf16[14,20,64,128]{3,2,0,1:T(8,128)(2,1)} fusion(bf16[7,20,64,64]{3,2,0,1:T(8,128)(2,1)S(1)} %concatenate.47, bf16[7,20,64,64]{3,2,0,1:T(8,128)(2,1)} %concatenate.46, bf16[7,20,64,64]{3,2,0,1:T(8,128)(2,1)} %concatenate.44, bf16[7,20,64,64]{3,2,0,1:T(8,128)(2,1)} %concatenate.43), kind=kLoop, calls=%fused_computation.6 | loop fusion | flops 18350080 | bytes 9175040 | tf_op jit(solution)/shard_map/concatenate | solution.py:71
  140.6 4.6 gather_fusion.3
  145.2 4.7 gather_fusion.1
  149.9 7.8 %select_select_fusion = (bf16[280,64,128]{2,1,0:T(8,128)(2,1)}, bf16[280,64,128]{2,1,0:T(8,128)(2,1)S(1)}) fusion(bf16[280,64,128]{2,1,0:T(8,128)(2,1)} %gather_fusion.3, pred[280]{0:T(512)(128)(4,1)S(1)} %compare_and_fusion, pred[280]{0:T(512)(128)(4,1)S(1)} %ge.42, bf16[280,64,128]{2,1,0:T(8,128)(2,1)} %gather_fusion.1), kind=kLoop, calls=%fused_computation.8 | loop fusion | flops 9175040 | bytes 18350640 | tf_op jit(solution)/shard_map/jit(_where)/select_n | solution.py:23
  159.3 4.7 gather_fusion
  164.0 4.7 select_select_fusion.3
  168.7 2.0 fusion.30
  170.7 4.9 fusion.8
  175.9 29.8 %scatter_fusion = f32[65,64,128]{2,1,0:T(8,128)S(1)} fusion(f32[65,64,128]{2,1,0:T(8,128)S(1)} %broadcast.48.clone, s32[280]{0:T(512)S(1)} %fusion.40, f32[280,64,128]{2,1,0:T(8,128)} %bitcast.77), kind=kCustom, calls=%fused_computation.4 | custom fusion | flops 2293760 | bytes 27526240 | tf_op jit(solution)/shard_map/scatter-add | solution.py:49
  207.9 147.0 %all-reduce.3.cloned.1.call-done = f32[4096,128]{1,0:T(8,128)} async-done(((f32[4096,128]{1,0:T(8,128)}), f32[4096,128]{1,0:T(8,128)}) %all-reduce.3.cloned.1.call-update) | async-done | bytes 2097168 | tf_op jit(solution)/shard_map/psum | solution.py:89
  358.0 6.1 %fusion.16 = f32[14,128,128]{2,1,0:T(8,128)} fusion(bf16[14,20,64,128]{3,2,1,0:T(8,128)(2,1)} %bitcast.84, bf16[14,20,64,128]{3,2,0,1:T(8,128)(2,1)} %maximum_maximum_fusion), kind=kOutput, calls=%fused_computation.27 | convolution fusion | flops 587202560 | bytes 10092544 | tf_op jit(solution)/shard_map/crkj,crkt->cjt/dot_general | solution.py:32
  364.1 34.7 %all-gather.13.cloned.1.call-done = bf16[1,1,4096,128]{3,2,1,0:T(8,128)(2,1)} async-done(((bf16[1,1,256,128]{3,2,1,0:T(8,128)(2,1)}), bf16[1,1,4096,128]{3,2,1,0:T(8,128)(2,1)}) %all-gather.13.cloned.1.call-update) | async-done | bytes 1048592 | tf_op jit(solution)/shard_map/all_gather | solution.py:84
  400.1 13.6 %gather_fusion.2 = bf16[280,64,128]{2,1,0:T(8,128)(2,1)} fusion(bf16[64,64,128]{2,1,0:T(8,128)(2,1)S(1)} %bitcast.78, s32[1024]{0:T(1024)S(1)} %pad_clamp_fusion.1), kind=kCustom, calls=%fused_computation.2.clone | custom fusion | bytes 9176160 | tf_op jit(solution)/shard_map/jit(_take)/gather | solution.py:22
  413.7 4.7 select_select_fusion.1
  418.5 2.0 fusion.27
  420.5 4.9 fusion.4
  425.7 29.8 %scatter_fusion.1 = f32[65,64,128]{2,1,0:T(8,128)S(1)} fusion(f32[65,64,128]{2,1,0:T(8,128)S(1)} %broadcast.48, s32[280]{0:T(512)S(1)} %fusion.40, f32[280,64,128]{2,1,0:T(8,128)} %bitcast.76), kind=kCustom, calls=%fused_computation.5 | custom fusion | flops 2293760 | bytes 27526240 | tf_op jit(solution)/shard_map/scatter-add | solution.py:49
  457.9 137.0 %all-reduce.5.cloned.1.call-done = f32[4096,128]{1,0:T(8,128)} async-done(((f32[4096,128]{1,0:T(8,128)}), f32[4096,128]{1,0:T(8,128)}) %all-reduce.5.cloned.1.call-update) | async-done | bytes 2097168 | tf_op jit(solution)/shard_map/psum | solution.py:89
  (82 shorter events, 22.3 us)
Async XLA Ops:
  6.5 134.1 %all-gather.15.cloned.1.call-start = ((), (), s32[]{:S(2)}) async-start(), calls=%async_computation.5 | async-start | bytes 1114112 | tf_op jit(solution)/shard_map/all_gather | solution.py:83
  8.1 137.1 %all-gather.11.cloned.1.call-start = ((), (), s32[]{:S(2)}) async-start(), calls=%async_computation.3 | async-start | bytes 1114112 | tf_op jit(solution)/shard_map/all_gather | solution.py:83
  8.8 150.5 %all-gather.9.cloned.1.call-start = ((), (), s32[]{:S(2)}) async-start(), calls=%async_computation.2 | async-start | bytes 1114112 | tf_op jit(solution)/shard_map/all_gather | solution.py:84
  9.6 20.7 %collective-permute-start = (s32[1,1,7,20]{3,2,1,0:T(8,128)S(1)}, s32[1,1,7,20]{3,2,1,0:T(8,128)S(1)}, u32[]{:S(2)}, u32[]{:S(2)}) collective-permute-start(s32[1,1,7,20]{3,2,1,0:T(8,128)S(1)} %copy.21), channel_id=1, source_target_pairs={{0,16},{16,0},{32,48},{48,32},{64,80},{80,64},{96,112},{112,96},{1... | collective-permute-start | bytes 1688 | tf_op jit(solution)/shard_map/ppermute | solution.py:10
  15.1 15.3 %collective-permute-start.4 = (s32[1,1,7,20]{3,1,2,0:T(1,128)}, s32[1,1,7,20]{3,1,2,0:T(1,128)S(1)}, u32[]{:S(2)}, u32[]{:S(2)}) collective-permute-start(s32[1,1,7,20]{3,1,2,0:T(1,128)} %param.15), channel_id=1, source_target_pairs={{0,16},{16,0},{32,48},{48,32},{64,80},{80,64},{96,112},{112,96},{1... | collective-permute-start | bytes 1688 | tf_op jit(solution)/shard_map/ppermute | solution.py:10
  17.0 34.3 %collective-permute-start.3 = (bf16[1,1,7,20,4096]{4,2,3,1,0:T(8,128)(2,1)}, bf16[1,1,7,20,4096]{4,2,3,1,0:T(8,128)(2,1)S(1)}, u32[]{:S(2)}, u32[]{:S(2)}) collective-permute-start(bf16[1,1,7,20,4096]{4,2,3,1,0:T(8,128)(2,1)} %param.13), channel_id=1, source_target_pairs={{0,16},{16,0},{32,48},{48,32},{64,80},{80,64},{96,112},{112,96},{1... | collective-permute-start | bytes 3440648 | tf_op jit(solution)/shard_map/ppermute | solution.py:10
  21.9 59.2 %collective-permute-start.2 = (bf16[1,1,7,20,4096]{4,2,3,1,0:T(8,128)(2,1)}, bf16[1,1,7,20,4096]{4,2,3,1,0:T(8,128)(2,1)S(1)}, u32[]{:S(2)}, u32[]{:S(2)}) collective-permute-start(bf16[1,1,7,20,4096]{4,2,3,1,0:T(8,128)(2,1)} %param.12), channel_id=1, source_target_pairs={{0,16},{16,0},{32,48},{48,32},{64,80},{80,64},{96,112},{112,96},{1... | collective-permute-start | bytes 3440648 | tf_op jit(solution)/shard_map/ppermute | solution.py:10
  23.8 88.9 %collective-permute-start.1 = (bf16[1,1,7,20,4096]{4,2,3,1,0:T(8,128)(2,1)}, bf16[1,1,7,20,4096]{4,2,3,1,0:T(8,128)(2,1)}, u32[]{:S(2)}, u32[]{:S(2)}) collective-permute-start(bf16[1,1,7,20,4096]{4,2,3,1,0:T(8,128)(2,1)} %param.11), channel_id=1, source_target_pairs={{0,16},{16,0},{32,48},{48,32},{64,80},{80,64},{96,112},{112,96},{1... | collective-permute-start | bytes 3440648 | tf_op jit(solution)/shard_map/ppermute | solution.py:10
  30.2 324.6 %all-reduce.3.cloned.1.call-start = ((), (), s32[]{:S(2)}) async-start(), calls=%async_computation | async-start | bytes 4194304 | tf_op jit(solution)/shard_map/psum | solution.py:89
  145.2 12.5 %slice-start = ((s8[4587520]{0:T(1024)(128)(4,1)}), s8[393216]{0:T(1024)(128)(4,1)S(1)}, s32[]{:S(2)}) async-start(s8[4587520]{0:T(1024)(128)(4,1)} %bitcast.70), calls=%async_computation.6 | async-start | bytes 786432
  149.9 7.8 %slice-start.1 = ((s8[4587520]{0:T(1024)(128)(4,1)}), s8[4194304]{0:T(1024)(128)(4,1)S(1)}, s32[]{:S(2)}) async-start(s8[4587520]{0:T(1024)(128)(4,1)} %bitcast.70), calls=%async_computation.7 | async-start | bytes 8388608
  163.9 4.7 copy-start.1
  164.0 4.7 copy-start.3
  164.0 6.8 %slice-start.2 = ((s8[4587520]{0:T(1024)(128)(4,1)}), s8[4194304]{0:T(1024)(128)(4,1)S(1)}, s32[]{:S(2)}) async-start(s8[4587520]{0:T(1024)(128)(4,1)} %bitcast.72), calls=%async_computation.8 | async-start | bytes 8388608
  168.7 2.0 slice-start.3
  205.7 149.1 %copy-start = (bf16[1,1,4096,128]{3,2,1,0:T(8,128)(2,1)S(1)}, bf16[1,1,4096,128]{3,2,1,0:T(8,128)(2,1)}, u32[]{:S(2)}) copy-start(bf16[1,1,4096,128]{3,2,1,0:T(8,128)(2,1)} %all-gather.9.cloned.1.call-done) | copy-start | bytes 3145732
  207.2 191.6 %all-gather.13.cloned.1.call-start = ((), (), s32[]{:S(2)}) async-start(), calls=%async_computation.4 | async-start | bytes 1114112 | tf_op jit(solution)/shard_map/all_gather | solution.py:84
  207.8 387.0 %all-reduce.5.cloned.1.call-start = ((), (), s32[]{:S(2)}) async-start(), calls=%async_computation.1 | async-start | bytes 4194304 | tf_op jit(solution)/shard_map/psum | solution.py:89
  356.7 7.4 %copy-start.5 = (bf16[4096,128]{1,0:T(8,128)(2,1)}, bf16[4096,128]{1,0:T(8,128)(2,1)S(1)}, u32[]{:S(2)}) copy-start(bf16[4096,128]{1,0:T(8,128)(2,1)S(1)} %fusion.12) | copy-start | bytes 3145732
  356.7 42.1 %collective-permute-start.5 = (bf16[4096,128]{1,0:T(8,128)(2,1)S(1)}, bf16[4096,128]{1,0:T(8,128)(2,1)S(1)}, u32[]{:S(2)}, u32[]{:S(2)}) collective-permute-start(bf16[4096,128]{1,0:T(8,128)(2,1)S(1)} %fusion.12), channel_id=1, source_target_pairs={{32,0},{48,16},{64,32},{80,48},{96,64},{112,80},{128,96},{144,112}... | collective-permute-start | bytes 3145736 | tf_op jit(solution)/shard_map/ppermute | solution.py:16
  400.1 18.3 %copy-start.6 = (f32[14,128,128]{2,1,0:T(8,128)S(1)}, f32[14,128,128]{2,1,0:T(8,128)}, u32[]{:S(2)}) copy-start(f32[14,128,128]{2,1,0:T(8,128)} %fusion.16) | copy-start | bytes 2752516
  413.7 4.8 copy-start.2
  413.7 4.8 copy-start.4
  413.7 6.8 %slice-start.4 = ((s8[4587520]{0:T(1024)(128)(4,1)}), s8[4194304]{0:T(1024)(128)(4,1)S(1)}, s32[]{:S(2)}) async-start(s8[4587520]{0:T(1024)(128)(4,1)} %bitcast.74), calls=%async_computation.10 | async-start | bytes 8388608
  418.5 2.0 slice-start.5
Sparse Core Ops, SparseCore 0:
  9.5 47.1 all-gather.14
  58.9 41.6 all-gather.10
  102.7 40.2 all-gather.8
  207.3 147.4 all-reduce.2
  356.8 41.8 all-gather.12
  457.1 137.6 all-reduce.4
where the time goes:
time: 606 us; the launch traced here: 603 us
  waiting for transfers between devices  389 us (64%)
  other arithmetic  96.3 us (16%)
  local copies, waits for them, and re-layouts  62.3 us (10%)
  matrix products  21.5 us (4%)
  starting transfers between devices  20.5 us (3%)
  between operations  14 us (2%)
    psum x2, waiting for transfers between devices, per_device(): summed = lax.psum(branch, 'tensor')  284 us
    ppermute x5, waiting for transfers between devices, partner_2(): lax.ppermute(x, axis, [(i, i ^ 1 << distance) for i in range(lax.axis_siz...  68.6 us
    scatter-add x2, other arithmetic, layer_branch(): jax.ops.segment_sum(per_slot.reshape(columns * slot_depth, BLK, tokens_no...  59.5 us
    all_gather x2, waiting for transfers between devices, per_device(): lax.all_gather(seed_panel, 'tensor', axis=0, tiled=True)  34.7 us
    gather x4, local copies, waits for them, and re-layouts, gather_tiles(): picked = jnp.take(source, jnp.maximum(row_ids, 0).reshape(-1), axis=0)  27.5 us
    concatenate x7, local copies, waits for them, and re-layouts, per_device(): jnp.concatenate([first_half[0, 0], second_half[0, 0]], axis=0)  26.4 us
    ppermute x5, starting transfers between devices, partner_2(): lax.ppermute(x, axis, [(i, i ^ 1 << distance) for i in range(lax.axis_siz...  19.1 us
    select_n x3, other arithmetic, gather_tiles(): picked = jnp.where(filled[:, None, None], picked, jnp.zeros_like(picked))  17.3 us
  transfers between devices with their start and end apart: 12, of which 6 were waited for; matrix products, arithmetic and copies ran while one was open for 12% of the time, Pallas kernels for 0%

commit v1 on v0

--- a/solution.py
+++ b/solution.py
@@ -4,6 +4,11 @@
 from jax.sharding import PartitionSpec as P
 
 BLK = 64
+
+
+def summed_here(x, axis):
+    parts = lax.all_gather(x, axis)
+    return jnp.sum(parts, axis=0)
 
 
 def partner_2(x, axis, distance):
@@ -86,7 +91,7 @@
         if micro_step > 0:
             cot_full = jnp.where(last_section, cot_full, arrived)
         branch = layer_branch(x_full, cot_full, paired_grid, down_grid, gate_ids, down_ids)
-        summed = lax.psum(branch, "tensor")
+        summed = summed_here(branch, "tensor")
         grad_full = (cot_full.astype(jnp.float32) + summed).astype(jnp.bfloat16)
         grad_panel = lax.dynamic_slice_in_dim(
             grad_full, lax.axis_index("tensor") * panel_rows, panel_rows, 0

time: 606 us -> 697 us (1.15)
  waiting for transfers between devices: 389 us -> 459 us
  other arithmetic: 96.3 us -> 118 us
    all_gather x0 -> x2, waiting for transfers between devices: none -> 365 us  [summed_here(): parts = lax.all_gather(x, axis)]
    psum x2 -> x0, waiting for transfers between devices: 284 us -> none  [per_device(): summed = lax.psum(branch, 'tensor')]
    reduce_sum x0 -> x2, other arithmetic: none -> 23.5 us  [summed_here(): return jnp.sum(parts, axis=0)]
    all_gather x2, waiting for transfers between devices: 34.7 us -> 23.8 us  [per_device(): lax.all_gather(seed_panel, 'tensor', axis=0, tiled=True)]
where the time goes in v1:
time: 697 us; the launch traced here: 694 us
  waiting for transfers between devices  459 us (66%)
  other arithmetic  118 us (17%)
  local copies, waits for them, and re-layouts  62.2 us (9%)
  starting transfers between devices  20.5 us (3%)
  matrix products  20.5 us (3%)
  between operations  14 us (2%)
    all_gather x2, waiting for transfers between devices, summed_here(): parts = lax.all_gather(x, axis)  365 us
    ppermute x5, waiting for transfers between devices, partner_2(): lax.ppermute(x, axis, [(i, i ^ 1 << distance) for i in range(lax.axis_siz...  68.7 us
    scatter-add x2, other arithmetic, layer_branch(): jax.ops.segment_sum(per_slot.reshape(columns * slot_depth, BLK, tokens_no...  59.5 us
    gather x4, local copies, waits for them, and re-layouts, gather_tiles(): picked = jnp.take(source, jnp.maximum(row_ids, 0).reshape(-1), axis=0)  27.5 us
    concatenate x7, local copies, waits for them, and re-layouts, per_device(): jnp.concatenate([first_half[0, 0], second_half[0, 0]], axis=0)  26.3 us
    all_gather x2, waiting for transfers between devices, per_device(): lax.all_gather(seed_panel, 'tensor', axis=0, tiled=True)  23.8 us
    reduce_sum x2, other arithmetic, summed_here(): return jnp.sum(parts, axis=0)  23.5 us
    ppermute x5, starting transfers between devices, partner_2(): lax.ppermute(x, axis, [(i, i ^ 1 << distance) for i in range(lax.axis_siz...  19.1 us
  transfers between devices with their start and end apart: 12, of which 6 were waited for; matrix products, arithmetic and copies ran while one was open for 12% of the time, Pallas kernels for 0%

profile of v1, /device:TPU:1, one launch (start us, length us, event | category | flops | bytes accessed | tf_op | source)
XLA Modules:
  0.0 694.4 jit_solution(15825447096296014825)
XLA Ops:
  9.6 5.5 collective-permute-start
  17.0 4.9 collective-permute-start.3
  23.8 4.9 collective-permute-start.1
  31.7 19.6 %collective-permute-done.3 = bf16[1,1,7,20,4096]{4,2,3,1,0:T(8,128)(2,1)S(1)} collective-permute-done((bf16[1,1,7,20,4096]{4,2,3,1,0:T(8,128)(2,1)}, bf16[1,1,7,20,4096]{4,2,3,1,0:T(8,128)(2,1)S(1)}, u32[]{:S(2)}, u32[]{:S(2)}) %collective-permute-start.3) | collective-permute-done | bytes 1146912 | tf_op jit(solution)/shard_map/ppermute | solution.py:15
  51.3 29.8 %collective-permute-done.2 = bf16[1,1,7,20,4096]{4,2,3,1,0:T(8,128)(2,1)S(1)} collective-permute-done((bf16[1,1,7,20,4096]{4,2,3,1,0:T(8,128)(2,1)}, bf16[1,1,7,20,4096]{4,2,3,1,0:T(8,128)(2,1)S(1)}, u32[]{:S(2)}, u32[]{:S(2)}) %collective-permute-start.2) | collective-permute-done | bytes 1146912 | tf_op jit(solution)/shard_map/ppermute | solution.py:15
  81.1 4.2 broadcast_select_fusion.1
  85.3 3.6 concatenate.47
  88.9 4.5 concatenate.46
  93.5 19.2 %collective-permute-done.1 = bf16[1,1,7,20,4096]{4,2,3,1,0:T(8,128)(2,1)} collective-permute-done((bf16[1,1,7,20,4096]{4,2,3,1,0:T(8,128)(2,1)}, bf16[1,1,7,20,4096]{4,2,3,1,0:T(8,128)(2,1)}, u32[]{:S(2)}, u32[]{:S(2)}) %collective-permute-start.1) | collective-permute-done | bytes 1146912 | tf_op jit(solution)/shard_map/ppermute | solution.py:15
  112.7 3.4 broadcast_select_fusion.5
  116.1 4.5 concatenate.44
  120.6 4.5 concatenate.43
  125.1 4.5 concatenate.51
  129.6 4.6 concatenate.50
  134.2 6.4 maximum_maximum_fusion
  140.5 4.6 gather_fusion.3
  145.2 4.7 gather_fusion.1
  149.9 7.8 %select_select_fusion = (bf16[280,64,128]{2,1,0:T(8,128)(2,1)}, bf16[280,64,128]{2,1,0:T(8,128)(2,1)S(1)}) fusion(bf16[280,64,128]{2,1,0:T(8,128)(2,1)} %gather_fusion.3, pred[280]{0:T(512)(128)(4,1)S(1)} %compare_and_fusion, pred[280]{0:T(512)(128)(4,1)S(1)} %ge.42, bf16[280,64,128]{2,1,0:T(8,128)(2,1)} %gather_fusion.1), kind=kLoop, calls=%fused_computation.8 | loop fusion | flops 9175040 | bytes 18350640 | tf_op jit(solution)/shard_map/jit(_where)/select_n | solution.py:28
  159.2 4.6 gather_fusion
  163.9 4.7 select_select_fusion.3
  170.7 4.9 fusion.8
  175.8 29.8 %scatter_fusion = f32[65,64,128]{2,1,0:T(8,128)S(1)} fusion(f32[65,64,128]{2,1,0:T(8,128)S(1)} %broadcast.48.clone, s32[280]{0:T(512)S(1)} %fusion.40, f32[280,64,128]{2,1,0:T(8,128)} %bitcast.77), kind=kCustom, calls=%fused_computation.4 | custom fusion | flops 2293760 | bytes 27526240 | tf_op jit(solution)/shard_map/scatter-add | solution.py:54
  207.7 187.6 %all-gather.11.cloned.1.call-done = f32[16,4096,128]{2,1,0:T(8,128)} async-done(((f32[1,4096,128]{2,1,0:T(8,128)}), f32[16,4096,128]{2,1,0:T(8,128)}) %all-gather.11.cloned.1.call-update) | async-done | bytes 33554448 | tf_op jit(solution)/shard_map/all_gather | solution.py:10
  395.3 11.7 %reduce_sum.18 = f32[4096,128]{1,0:T(8,128)S(1)} reduce(f32[16,4096,128]{2,1,0:T(8,128)} %all-gather.11.cloned.1.call-done, f32[]{:T(128)} %constant.26.clone.1), dimensions={0}, to_apply=%region_1.3 | reduce | flops 7864320 | bytes 35651588 | tf_op jit(solution)/shard_map/reduce_sum | solution.py:11
  409.6 5.1 fusion.16
  414.7 23.8 %all-gather.19.cloned.1.call-done = bf16[1,1,4096,128]{3,2,1,0:T(8,128)(2,1)} async-done(((bf16[1,1,256,128]{3,2,1,0:T(8,128)(2,1)}), bf16[1,1,4096,128]{3,2,1,0:T(8,128)(2,1)}) %all-gather.19.cloned.1.call-update) | async-done | bytes 1048592 | tf_op jit(solution)/shard_map/all_gather | solution.py:89
  439.8 13.6 %gather_fusion.2 = bf16[280,64,128]{2,1,0:T(8,128)(2,1)} fusion(bf16[64,64,128]{2,1,0:T(8,128)(2,1)S(1)} %bitcast.78, s32[1024]{0:T(1024)S(1)} %pad_clamp_fusion.1), kind=kCustom, calls=%fused_computation.2.clone | custom fusion | bytes 9176160 | tf_op jit(solution)/shard_map/jit(_take)/gather | solution.py:27
  453.4 4.7 select_select_fusion.1
  460.2 4.9 fusion.4
  465.4 29.8 %scatter_fusion.1 = f32[65,64,128]{2,1,0:T(8,128)S(1)} fusion(f32[65,64,128]{2,1,0:T(8,128)S(1)} %broadcast.48, s32[280]{0:T(512)S(1)} %fusion.40, f32[280,64,128]{2,1,0:T(8,128)} %bitcast.76), kind=kCustom, calls=%fused_computation.5 | custom fusion | flops 2293760 | bytes 27526240 | tf_op jit(solution)/shard_map/scatter-add | solution.py:54
  497.5 177.6 %all-gather.13.cloned.1.call-done = f32[16,4096,128]{2,1,0:T(8,128)} async-done(((f32[1,4096,128]{2,1,0:T(8,128)}), f32[16,4096,128]{2,1,0:T(8,128)}) %all-gather.13.cloned.1.call-update) | async-done | bytes 33554448 | tf_op jit(solution)/shard_map/all_gather | solution.py:10
  675.1 11.7 %reduce_sum.19 = f32[4096,128]{1,0:T(8,128)S(1)} reduce(f32[16,4096,128]{2,1,0:T(8,128)} %all-gather.13.cloned.1.call-done, f32[]{:T(128)} %constant.26.clone.1), dimensions={0}, to_apply=%region_3.5 | reduce | flops 7864320 | bytes 35651588 | tf_op jit(solution)/shard_map/reduce_sum | solution.py:11
  (80 shorter events, 24.6 us)
Async XLA Ops:
  6.5 134.0 %all-gather.21.cloned.1.call-start = ((), (), s32[]{:S(2)}) async-start(), calls=%async_computation.5 | async-start | bytes 1114112 | tf_op jit(solution)/shard_map/all_gather | solution.py:88
  8.1 137.1 %all-gather.17.cloned.1.call-start = ((), (), s32[]{:S(2)}) async-start(), calls=%async_computation.3 | async-start | bytes 1114112 | tf_op jit(solution)/shard_map/all_gather | solution.py:88
  8.8 150.4 %all-gather.15.cloned.1.call-start = ((), (), s32[]{:S(2)}) async-start(), calls=%async_computation.2 | async-start | bytes 1114112 | tf_op jit(solution)/shard_map/all_gather | solution.py:89
  9.6 20.7 %collective-permute-start = (s32[1,1,7,20]{3,2,1,0:T(8,128)S(1)}, s32[1,1,7,20]{3,2,1,0:T(8,128)S(1)}, u32[]{:S(2)}, u32[]{:S(2)}) collective-permute-start(s32[1,1,7,20]{3,2,1,0:T(8,128)S(1)} %copy.33), channel_id=1, source_target_pairs={{0,16},{16,0},{32,48},{48,32},{64,80},{80,64},{96,112},{112,96},{1... | collective-permute-start | bytes 1688 | tf_op jit(solution)/shard_map/ppermute | solution.py:15
  15.0 15.2 %collective-permute-start.4 = (s32[1,1,7,20]{3,1,2,0:T(1,128)}, s32[1,1,7,20]{3,1,2,0:T(1,128)S(1)}, u32[]{:S(2)}, u32[]{:S(2)}) collective-permute-start(s32[1,1,7,20]{3,1,2,0:T(1,128)} %param.15), channel_id=1, source_target_pairs={{0,16},{16,0},{32,48},{48,32},{64,80},{80,64},{96,112},{112,96},{1... | collective-permute-start | bytes 1688 | tf_op jit(solution)/shard_map/ppermute | solution.py:15
  17.0 34.3 %collective-permute-start.3 = (bf16[1,1,7,20,4096]{4,2,3,1,0:T(8,128)(2,1)}, bf16[1,1,7,20,4096]{4,2,3,1,0:T(8,128)(2,1)S(1)}, u32[]{:S(2)}, u32[]{:S(2)}) collective-permute-start(bf16[1,1,7,20,4096]{4,2,3,1,0:T(8,128)(2,1)} %param.13), channel_id=1, source_target_pairs={{0,16},{16,0},{32,48},{48,32},{64,80},{80,64},{96,112},{112,96},{1... | collective-permute-start | bytes 3440648 | tf_op jit(solution)/shard_map/ppermute | solution.py:15
  21.9 59.2 %collective-permute-start.2 = (bf16[1,1,7,20,4096]{4,2,3,1,0:T(8,128)(2,1)}, bf16[1,1,7,20,4096]{4,2,3,1,0:T(8,128)(2,1)S(1)}, u32[]{:S(2)}, u32[]{:S(2)}) collective-permute-start(bf16[1,1,7,20,4096]{4,2,3,1,0:T(8,128)(2,1)} %param.12), channel_id=1, source_target_pairs={{0,16},{16,0},{32,48},{48,32},{64,80},{80,64},{96,112},{112,96},{1... | collective-permute-start | bytes 3440648 | tf_op jit(solution)/shard_map/ppermute | solution.py:15
  23.8 88.9 %collective-permute-start.1 = (bf16[1,1,7,20,4096]{4,2,3,1,0:T(8,128)(2,1)}, bf16[1,1,7,20,4096]{4,2,3,1,0:T(8,128)(2,1)}, u32[]{:S(2)}, u32[]{:S(2)}) collective-permute-start(bf16[1,1,7,20,4096]{4,2,3,1,0:T(8,128)(2,1)} %param.11), channel_id=1, source_target_pairs={{0,16},{16,0},{32,48},{48,32},{64,80},{80,64},{96,112},{112,96},{1... | collective-permute-start | bytes 3440648 | tf_op jit(solution)/shard_map/ppermute | solution.py:15
  30.2 365.1 %all-gather.11.cloned.1.call-start = ((), (), s32[]{:S(2)}) async-start(), calls=%async_computation | async-start | bytes 35651584 | tf_op jit(solution)/shard_map/all_gather | solution.py:10
  145.2 12.5 %slice-start = ((s8[4587520]{0:T(1024)(128)(4,1)}), s8[393216]{0:T(1024)(128)(4,1)S(1)}, s32[]{:S(2)}) async-start(s8[4587520]{0:T(1024)(128)(4,1)} %bitcast.70), calls=%async_computation.6 | async-start | bytes 786432
  149.9 7.8 %slice-start.1 = ((s8[4587520]{0:T(1024)(128)(4,1)}), s8[4194304]{0:T(1024)(128)(4,1)S(1)}, s32[]{:S(2)}) async-start(s8[4587520]{0:T(1024)(128)(4,1)} %bitcast.70), calls=%async_computation.7 | async-start | bytes 8388608
  163.9 4.7 copy-start.1
  163.9 4.7 copy-start.3
  163.9 6.8 slice-start.2
  168.6 2.0 slice-start.3
  207.1 231.4 %all-gather.19.cloned.1.call-start = ((), (), s32[]{:S(2)}) async-start(), calls=%async_computation.4 | async-start | bytes 1114112 | tf_op jit(solution)/shard_map/all_gather | solution.py:89
  207.7 199.4 %copy-start = (bf16[1,1,4096,128]{3,2,1,0:T(8,128)(2,1)S(1)}, bf16[1,1,4096,128]{3,2,1,0:T(8,128)(2,1)}, u32[]{:S(2)}) copy-start(bf16[1,1,4096,128]{3,2,1,0:T(8,128)(2,1)} %all-gather.15.cloned.1.call-done) | copy-start | bytes 3145732
  207.7 467.5 %all-gather.13.cloned.1.call-start = ((), (), s32[]{:S(2)}) async-start(), calls=%async_computation.1 | async-start | bytes 35651584 | tf_op jit(solution)/shard_map/all_gather | solution.py:10
  408.3 30.2 %collective-permute-start.5 = (bf16[4096,128]{1,0:T(8,128)(2,1)}, bf16[4096,128]{1,0:T(8,128)(2,1)S(1)}, u32[]{:S(2)}, u32[]{:S(2)}) collective-permute-start(bf16[4096,128]{1,0:T(8,128)(2,1)} %fusion.12), channel_id=1, source_target_pairs={{32,0},{48,16},{64,32},{80,48},{96,64},{112,80},{128,96},{144,112}... | collective-permute-start | bytes 3145736 | tf_op jit(solution)/shard_map/ppermute | solution.py:21
  453.4 4.8 copy-start.2
  453.4 4.8 copy-start.4
  453.4 6.8 slice-start.4
  458.2 2.0 slice-start.5
Sparse Core Ops, SparseCore 0:
  9.5 47.1 all-gather.20
  58.9 41.6 all-gather.16
  102.7 40.2 all-gather.14
  207.2 188.1 all-gather.10
  397.3 41.1 all-gather.18
  496.8 178.3 all-gather.12
